TPU v7x, 32 devices: a whole 2x2x4 slice. The times are simulated.
32 devices in a mesh: seq: 8 (over y, x, core), rep: 4 (over z).
Axes of the slice: x: 2, y: 2, z: 4, core: 2. Of those that a mesh axis runs over, the one named last changes fastest.
Arguments:
- out_grad: bfloat16 [4, 16, 131072], P('rep', None, 'seq'), may hold values from -6 to 6
- gate_act: bfloat16 [4, 16, 131072], P('rep', None, 'seq'), may hold values from -6 to 6
- conv_out: bfloat16 [4, 16, 131072], P('rep', None, 'seq'), may hold values from -6 to 6
- value_act: bfloat16 [4, 16, 131072], P('rep', None, 'seq'), may hold values from -6 to 6
- filter_taps: float32 [131072], P('seq'), may hold values from -1 to 1
- skip_gain: float32 [16], replicated, may hold values from 0.25 to 1.75
Outputs:
- gate_grad: bfloat16 [4, 16, 131072], P('rep', None, 'seq')
- value_grad: bfloat16 [4, 16, 131072], P('rep', None, 'seq')
- filter_grad: float32 [131072], P('seq')
All inputs are finite; a program needn't handle non-finite values.
Results may differ from a plain program's by a relative error of at most 0.001.
Values sent between devices are 32-bit elements; how exact they have to be, the bound alone decides.
No kernel may reach another device: no remote copies, remote signals or barrier semaphores. Data moves between devices by JAX's collectives and lax.ppermute only.
A program may use at most 128 MiB of HBM per device.

v0:
```python
import math

import jax
import jax.numpy as jnp
from jax import lax
from jax.sharding import PartitionSpec as P

HIGHEST = lax.Precision.HIGHEST


def unit_table(product, modulus):
    phase_rad = (product % modulus).astype(jnp.float32) * (-2.0 * math.pi / modulus)
    return (jnp.cos(phase_rad), jnp.sin(phase_rad))


def middle_mix(table, values):
    lead_dims = values.shape[:-2]
    flat = values.reshape((-1,) + values.shape[-2:])
    tiled = jnp.broadcast_to(table[None], (flat.shape[0],) + table.shape)
    result = jnp.einsum("rka,rab->rkb", tiled, flat, precision=HIGHEST)
    return result.reshape(lead_dims + result.shape[-2:])


def middle_complex(left_re, left_im, table_re, table_im):
    out_re = middle_mix(table_re, left_re) - middle_mix(table_im, left_im)
    out_im = middle_mix(table_im, left_re) + middle_mix(table_re, left_im)
    return (out_re, out_im)


def last_complex(form, left_re, left_im, table_re, table_im):
    out_re = jnp.einsum(form, left_re, table_re, precision=HIGHEST) - jnp.einsum(
        form, left_im, table_im, precision=HIGHEST
    )
    out_im = jnp.einsum(form, left_re, table_im, precision=HIGHEST) + jnp.einsum(
        form, left_im, table_re, precision=HIGHEST
    )
    return (out_re, out_im)


def row_order(seq_count):
    slot_ids = jnp.arange(2 * seq_count, dtype=jnp.int32)
    owner_dev = slot_ids // 2
    second = jnp.where(owner_dev == 0, seq_count, 2 * seq_count - owner_dev)
    return jnp.where(slot_ids % 2 == 0, owner_dev, second)


def cross_forward(pieces):
    seq_count = pieces.shape[1]
    block_len = pieces.shape[2]
    modulus = 2 * seq_count * seq_count * block_len
    freq_rows = row_order(seq_count)
    sources = jnp.arange(seq_count, dtype=jnp.int32)
    table_re, table_im = unit_table(freq_rows[:, None] * sources[None, :], 2 * seq_count)
    mixed_re = middle_mix(table_re, pieces)
    mixed_im = middle_mix(table_im, pieces)
    offsets = lax.axis_index("seq") * block_len + jnp.arange(block_len, dtype=jnp.int32)
    twist_re, twist_im = unit_table(freq_rows[:, None] * offsets[None, :], modulus)
    return (mixed_re * twist_re - mixed_im * twist_im, mixed_re * twist_im + mixed_im * twist_re)


def cross_inverse(operands):
    re_part, im_part = operands
    seq_count = re_part.shape[1] // 2
    block_len = re_part.shape[2]
    modulus = 2 * seq_count * seq_count * block_len
    freq_rows = row_order(seq_count)
    offsets = lax.axis_index("seq") * block_len + jnp.arange(block_len, dtype=jnp.int32)
    twist_re, twist_im = unit_table(freq_rows[:, None] * offsets[None, :], modulus)
    re_part, im_part = (
        re_part * twist_re + im_part * twist_im,
        im_part * twist_re - re_part * twist_im,
    )
    sources = jnp.arange(seq_count, dtype=jnp.int32)
    table_re, table_im = unit_table(sources[:, None] * freq_rows[None, :], 2 * seq_count)
    out_re = middle_mix(table_re, re_part) + middle_mix(table_im, im_part)
    return out_re


def local_forward(operands):
    re_part, im_part = operands
    lead_dims = re_part.shape[:-1]
    length_s = re_part.shape[-1]
    rows_a = length_s // 128
    re_part = re_part.reshape(lead_dims + (rows_a, 128))
    im_part = im_part.reshape(lead_dims + (rows_a, 128))
    steps_a = jnp.arange(rows_a, dtype=jnp.int32)
    steps_b = jnp.arange(128, dtype=jnp.int32)
    first_re, first_im = unit_table(steps_a[:, None] * steps_a[None, :], rows_a)
    re_part, im_part = middle_complex(re_part, im_part, first_re, first_im)
    twist_re, twist_im = unit_table(steps_a[:, None] * steps_b[None, :], length_s)
    re_part, im_part = (
        re_part * twist_re - im_part * twist_im,
        re_part * twist_im + im_part * twist_re,
    )
    last_re, last_im = unit_table(steps_b[:, None] * steps_b[None, :], 128)
    return last_complex("...kb,bl->...kl", re_part, im_part, last_re, last_im)


def local_inverse(re_part, im_part):
    lead_dims = re_part.shape[:-2]
    rows_a = re_part.shape[-2]
    length_s = rows_a * 128
    steps_a = jnp.arange(rows_a, dtype=jnp.int32)
    steps_b = jnp.arange(128, dtype=jnp.int32)
    last_re, last_im = unit_table(steps_b[:, None] * steps_b[None, :], 128)
    re_part, im_part = last_complex("...kl,bl->...kb", re_part, im_part, last_re, -last_im)
    twist_re, twist_im = unit_table(steps_a[:, None] * steps_b[None, :], length_s)
    re_part, im_part = (
        re_part * twist_re + im_part * twist_im,
        im_part * twist_re - re_part * twist_im,
    )
    first_re, first_im = unit_table(steps_a[:, None] * steps_a[None, :], rows_a)
    re_part, im_part = middle_complex(re_part, im_part, first_re, -first_im)
    return (re_part.reshape(lead_dims + (length_s,)), im_part.reshape(lead_dims + (length_s,)))


def local(out_grad, gate_act, conv_out, value_act, filter_taps, skip_gain):
    batch_rows = out_grad.shape[0]
    channels = out_grad.shape[1]
    length_s = out_grad.shape[2]
    seq_count = lax.axis_size("seq")
    row_total = batch_rows * channels
    gated_rows = out_grad.astype(jnp.float32) * gate_act.astype(jnp.float32)
    gate_grad = (out_grad.astype(jnp.float32) * conv_out.astype(jnp.float32)).astype(jnp.bfloat16)
    stacked = jnp.concatenate(
        [
            gated_rows.reshape(row_total, length_s),
            value_act.astype(jnp.float32).reshape(row_total, length_s),
            filter_taps.reshape(1, length_s),
        ],
        axis=0,
    )
    mixed_re, mixed_im = cross_forward(
        lax.all_to_all(
            stacked.reshape(2 * row_total + 1, 1, length_s),
            "seq",
            split_axis=2,
            concat_axis=1,
            tiled=True,
        )
    )
    spec_re, spec_im = local_forward(
        (
            lax.all_to_all(mixed_re, "seq", split_axis=1, concat_axis=2, tiled=True),
            lax.all_to_all(mixed_im, "seq", split_axis=1, concat_axis=2, tiled=True),
        )
    )
    grad_re = spec_re[:row_total]
    grad_im = spec_im[:row_total]
    value_re = spec_re[row_total : 2 * row_total]
    value_im = spec_im[row_total : 2 * row_total]
    filt_re = spec_re[2 * row_total]
    filt_im = spec_im[2 * row_total]
    carry_re = filt_re * grad_re + filt_im * grad_im
    carry_im = filt_re * grad_im - filt_im * grad_re
    lag_re = jnp.sum(grad_re * value_re + grad_im * value_im, axis=0)
    lag_im = jnp.sum(grad_im * value_re - grad_re * value_im, axis=0)
    lag_re, lag_im = lax.psum((lag_re, lag_im), "rep")
    back_re, back_im = local_inverse(
        jnp.concatenate([carry_re, lag_re[None]], axis=0),
        jnp.concatenate([carry_im, lag_im[None]], axis=0),
    )
    rows_out = cross_inverse(
        (
            lax.all_to_all(back_re, "seq", split_axis=2, concat_axis=1, tiled=True),
            lax.all_to_all(back_im, "seq", split_axis=2, concat_axis=1, tiled=True),
        )
    )
    rows_time = lax.all_to_all(rows_out, "seq", split_axis=1, concat_axis=2, tiled=True)
    rows_time = rows_time.reshape(row_total + 1, length_s) * (1.0 / (2 * seq_count * length_s))
    carried = rows_time[:row_total].reshape(batch_rows, channels, length_s)
    value_grad = (carried + skip_gain[None, :, None] * gated_rows).astype(jnp.bfloat16)
    lag_taps = rows_time[row_total]
    norm_scale = 1.0 / math.sqrt(
        batch_rows * lax.axis_size("rep") * channels * length_s * seq_count
    )
    filter_grad = lag_taps * norm_scale
    return (gate_grad, value_grad, filter_grad)


def solution(mesh):
    return jax.shard_map(
        local,
        mesh=mesh,
        in_specs=(
            P("rep", None, "seq"),
            P("rep", None, "seq"),
            P("rep", None, "seq"),
            P("rep", None, "seq"),
            P("seq"),
            P(),
        ),
        out_specs=(P("rep", None, "seq"), P("rep", None, "seq"), P("seq")),
        check_vma=False,
    )
```

profile of v0, /device:TPU:0, one launch (start us, length us, event | category | flops | bytes accessed | tf_op | source)
XLA Modules:
  0.0 709.1 jit_solution(3196688340106611680)
XLA Ops:
  15.1 74.5 %reduce = f32[16384,33]{1,0:T(8,128)} reduce(f32[16384,1,33]{2,1,0:T(1,128)} %bitcast.95, f32[]{:T(128)} %broadcast.616), dimensions={1}, to_apply=%bitcast.60.reduce_sub_computation | reduce | bytes 4325380
  89.6 11.2 %reshape.394 = f32[8,1,67584]{2,1,0:T(1,128)} reshape(f32[16384,33]{1,0:T(8,128)} %reduce) | data formatting | bytes 4325376
  106.8 26.6 %all-to-all-done = f32[8,1,67584]{2,1,0:T(1,128)} async-done(((f32[8,1,67584]{2,1,0:T(1,128)}), f32[8,1,67584]{2,1,0:T(1,128)}, u32[]{:S(2)}, u32[]{:S(2)}) %all-to-all-start) | async-done | bytes 2162720 | tf_op jit(solution)/shard_map/all_to_all | solution.py:134
  133.4 7.4 %reduce.1 = f32[8,67584]{1,0:T(8,128)S(1)} reduce(f32[8,1,67584]{2,1,0:T(1,128)} %all-to-all-done, f32[]{:T(128)} %broadcast.616), dimensions={1}, to_apply=%all_to_all.64.reduce_sub_computation | reduce | bytes 4325380 | tf_op jit(solution)/shard_map/all_to_all | solution.py:134
  140.8 20.0 %reshape.395 = f32[16384,1,33]{2,1,0:T(1,128)} reshape(f32[8,67584]{1,0:T(8,128)S(1)} %reduce.1) | data formatting | bytes 4325376
  170.1 6.4 multiply_add_fusion.1
  186.1 7.1 %copy.65 = f32[33,16,2048]{2,0,1:T(8,128)} copy(f32[33,16,2048]{2,1,0:T(8,128)} %get-tuple-element.16) | data formatting | bytes 8650752 | tf_op jit(solution)/shard_map/sub | solution.py:58
  193.2 53.3 %all-to-all-done.2 = f32[33,16,2048]{2,0,1:T(8,128)} async-done(((f32[33,16,2048]{2,0,1:T(8,128)}), f32[33,16,2048]{2,0,1:T(8,128)}, u32[]{:S(2)}, u32[]{:S(2)}) %all-to-all-start.2) | async-done | bytes 4325408 | tf_op jit(solution)/shard_map/all_to_all | solution.py:145
  252.0 7.0 copy.81
  264.3 47.2 %all-to-all-done.1 = f32[33,16,2048]{2,0,1:T(8,128)} async-done(((f32[33,16,2048]{2,0,1:T(8,128)}), f32[33,16,2048]{2,0,1:T(8,128)}, u32[]{:S(2)}, u32[]{:S(2)}) %all-to-all-start.1) | async-done | bytes 4325408 | tf_op jit(solution)/shard_map/all_to_all | solution.py:144
  311.5 7.0 copy.82
  323.8 6.2 fusion.7
  364.6 35.4 %all-reduce.3.cloned.1.call-done = (f32[1,2,128,128]{3,2,1,0:T(8,128)}, f32[1,2,128,128]{3,2,1,0:T(8,128)}) async-done(((f32[1,2,128,128]{3,2,1,0:T(8,128)}, f32[1,2,128,128]{3,2,1,0:T(8,128)}), (f32[1,2,128,128]{3,2,1,0:T(8,128)}, f32[1,2,128,128]{3,2,1,0:T(8,128)})) %all-reduce.3.cloned.1.call-update) | async-done | bytes 262160 | tf_op jit(solution)/shard_map/psum | solution.py:158
  422.7 18.8 %copy.71 = f32[17,2,16384]{0,1,2:T(2,128)} copy(f32[17,2,16384]{2,1,0:T(2,128)} %add.234) | data formatting | bytes 4456448 | tf_op jit(solution)/shard_map/add | solution.py:26
  441.5 27.5 %reshape.396 = f32[8,1,69632]{2,1,0:T(1,128)} reshape(f32[16384,2,17]{2,1,0:T(2,128)} %bitcast.88) | data formatting | bytes 4456448
  483.7 15.1 %copy.69 = f32[17,2,16384]{0,1,2:T(2,128)} copy(f32[17,2,16384]{2,1,0:T(2,128)S(1)} %sub.82) | data formatting | bytes 4456448 | tf_op jit(solution)/shard_map/sub | solution.py:25
  498.8 27.5 %reshape.398 = f32[8,1,69632]{2,1,0:T(1,128)} reshape(f32[16384,2,17]{2,1,0:T(2,128)} %bitcast.89) | data formatting | bytes 4456448
  530.9 7.6 %reduce.2 = f32[8,69632]{1,0:T(8,128)S(1)} reduce(f32[8,1,69632]{2,1,0:T(1,128)} %all-to-all-done.4, f32[]{:T(128)} %broadcast.616), dimensions={1}, to_apply=%all_to_all.76.reduce_sub_computation | reduce | bytes 4456452 | tf_op jit(solution)/shard_map/all_to_all | solution.py:166
  538.5 32.8 %reshape.397 = f32[16384,2,17]{2,1,0:T(2,128)} reshape(f32[8,69632]{1,0:T(8,128)S(1)} %reduce.2) | data formatting | bytes 4456448
  571.3 22.0 %copy.72 = f32[17,8,2,2048]{3,2,1,0:T(2,128)} copy(f32[17,8,2,2048]{0,2,3,1:T(2,128)} %bitcast.90) | data formatting | bytes 4456448 | tf_op jit(solution)/shard_map/all_to_all | solution.py:166
  596.4 8.9 %reduce.3 = f32[8,69632]{1,0:T(8,128)} reduce(f32[8,1,69632]{2,1,0:T(1,128)} %all-to-all-done.3, f32[]{:T(128)} %broadcast.616), dimensions={1}, to_apply=%all_to_all.72.reduce_sub_computation | reduce | bytes 4456452 | tf_op jit(solution)/shard_map/all_to_all | solution.py:165
  605.4 35.9 %reshape.399 = f32[16384,2,17]{2,1,0:T(2,128)} reshape(f32[8,69632]{1,0:T(8,128)} %reduce.3) | data formatting | bytes 4456448
  641.2 22.0 %copy.70 = f32[17,8,2,2048]{3,2,1,0:T(2,128)} copy(f32[17,8,2,2048]{0,2,3,1:T(2,128)} %bitcast.91) | data formatting | bytes 4456448 | tf_op jit(solution)/shard_map/all_to_all | solution.py:165
  672.6 24.9 %all_to_all.87 = f32[17,8,2048]{2,0,1:T(8,128)S(1)} all-to-all(f32[17,8,2048]{2,0,1:T(8,128)S(1)} %copy.73), channel_id=1, replica_groups=mesh['seq'=8,'rep'=4] {'seq'}, dimensions={1} | all-to-all | bytes 2228224 | tf_op jit(solution)/shard_map/all_to_all | solution.py:169
  (86 shorter events, 142.3 us)
Async XLA Ops:
  7.2 2.5 copy-start.9
  100.7 32.6 %all-to-all-start = ((f32[8,1,67584]{2,1,0:T(1,128)}), f32[8,1,67584]{2,1,0:T(1,128)}, u32[]{:S(2)}, u32[]{:S(2)}) async-start(f32[8,1,67584]{2,1,0:T(1,128)} %reshape.394), calls=%async_computation | async-start | bytes 4325376 | tf_op jit(solution)/shard_map/all_to_all | solution.py:134
  181.4 65.0 %all-to-all-start.2 = ((f32[33,16,2048]{2,0,1:T(8,128)}), f32[33,16,2048]{2,0,1:T(8,128)}, u32[]{:S(2)}, u32[]{:S(2)}) async-start(f32[33,16,2048]{2,0,1:T(8,128)} %copy.67), calls=%async_computation.2 | async-start | bytes 10485760 | tf_op jit(solution)/shard_map/all_to_all | solution.py:145
  246.4 65.0 %all-to-all-start.1 = ((f32[33,16,2048]{2,0,1:T(8,128)}), f32[33,16,2048]{2,0,1:T(8,128)}, u32[]{:S(2)}, u32[]{:S(2)}) async-start(f32[33,16,2048]{2,0,1:T(8,128)} %copy.65), calls=%async_computation.1 | async-start | bytes 10485760 | tf_op jit(solution)/shard_map/all_to_all | solution.py:144
  251.1 148.8 %all-reduce.3.cloned.1.call-start = ((), (), s32[]{:S(2)}) async-start(), calls=%async_computation.6 | async-start | bytes 524288 | tf_op jit(solution)/shard_map/psum | solution.py:158
  323.8 6.2 copy-start
  323.8 10.7 %slice-start = ((s8[4325376]{0:T(1024)(128)(4,1)}), s8[4194304]{0:T(1024)(128)(4,1)S(1)}, s32[]{:S(2)}) async-start(s8[4325376]{0:T(1024)(128)(4,1)} %bitcast.92), calls=%async_computation.7 | async-start | bytes 8388608
  330.0 4.5 slice-start.1
  364.3 41.9 %copy-start.3 = (f32[16,2,128,128]{3,2,1,0:T(8,128)}, f32[16,2,128,128]{3,2,1,0:T(8,128)S(1)}, u32[]{:S(2)}) copy-start(f32[16,2,128,128]{3,2,1,0:T(8,128)S(1)} %get-tuple-element.13) | copy-start | bytes 6291460
  400.0 4.0 copy-start.4
  400.0 4.0 copy-start.8
  404.0 2.2 copy-start.7
  413.2 2.2 copy-start.2
  469.0 57.3 %all-to-all-start.4 = ((f32[8,1,69632]{2,1,0:T(1,128)}), f32[8,1,69632]{2,1,0:T(1,128)}, u32[]{:S(2)}, u32[]{:S(2)}) async-start(f32[8,1,69632]{2,1,0:T(1,128)} %reshape.396), calls=%async_computation.4 | async-start | bytes 4456448 | tf_op jit(solution)/shard_map/all_to_all | solution.py:166
  526.3 70.1 %all-to-all-start.3 = ((f32[8,1,69632]{2,1,0:T(1,128)}), f32[8,1,69632]{2,1,0:T(1,128)}, u32[]{:S(2)}, u32[]{:S(2)}) async-start(f32[8,1,69632]{2,1,0:T(1,128)} %reshape.398), calls=%async_computation.3 | async-start | bytes 4456448 | tf_op jit(solution)/shard_map/all_to_all | solution.py:165
  667.2 3.2 copy-start.1
  698.5 1.0 copy-start.5
  698.5 1.2 copy-start.6
  698.5 1.2 copy-start.10
Sparse Core Ops, SparseCore 0:
  364.5 35.4 all-reduce.2
where the time goes:
time: 718 us; the launch traced here: 709 us
  local copies, waits for them, and re-layouts  296 us (41%)
  waiting for transfers between devices  162 us (23%)
  other arithmetic  109 us (15%)
  matrix products  78.3 us (11%)
  blocking collectives  24.9 us (3%)
  starting transfers between devices  23.8 us (3%)
  between operations  14.8 us (2%)
    unnamed x33, local copies, waits for them, and re-layouts  156 us
    unnamed x2, other arithmetic  74.5 us
    all_to_all x1, waiting for transfers between devices, local(): lax.all_to_all(mixed_im, 'seq', split_axis=1, concat_axis=2, tiled=True)  53.3 us
    dot_general x12, matrix products, middle_mix(): result = jnp.einsum('rka,rab->rkb', tiled, flat, precision=HIGHEST)  48 us
    all_to_all x1, waiting for transfers between devices, local(): lax.all_to_all(mixed_re, 'seq', split_axis=1, concat_axis=2, tiled=True)  47.2 us
    psum x1, waiting for transfers between devices, local(): lag_re, lag_im = lax.psum((lag_re, lag_im), 'rep')  35.4 us
    all_to_all x1, waiting for transfers between devices, local(): lax.all_to_all(stacked.reshape(2 * row_total + 1, 1, length_s), 'seq', sp...  26.6 us
    all_to_all x2, local copies, waits for them, and re-layouts, local(): lax.all_to_all(back_re, 'seq', split_axis=2, concat_axis=1, tiled=True)  26 us
  transfers between devices with their start and end apart: 6, of which 4 were waited for; matrix products, arithmetic and copies ran while one was open for 19% of the time, Pallas kernels for 0%

commit v1 on v0

v1 whole, which is shorter than its diff:
```python
import math

import jax
import jax.numpy as jnp
from jax import lax
from jax.sharding import PartitionSpec as P

HIGHEST = lax.Precision.HIGHEST
LANES = 128


def unit_table(product, modulus):
    phase_rad = (product % modulus).astype(jnp.float32) * (-2.0 * math.pi / modulus)
    return (jnp.cos(phase_rad), jnp.sin(phase_rad))


def row_order(seq_count):
    slot_ids = jnp.arange(2 * seq_count, dtype=jnp.int32)
    owner_dev = slot_ids // 2
    second = jnp.where(owner_dev == 0, seq_count, 2 * seq_count - owner_dev)
    return jnp.where(slot_ids % 2 == 0, owner_dev, second)


def lmul(table, values):
    return jnp.tensordot(table, values, axes=1, precision=HIGHEST)


def rmul(values, table):
    return jnp.tensordot(values, table, axes=1, precision=HIGHEST)


def swap_leading(values):
    return lax.all_to_all(values, "seq", split_axis=0, concat_axis=0, tiled=True)


def local_inverse(spec_re, spec_im, seq_count, slot_freq, offsets, modulus):
    rows_a = spec_re.shape[0]
    length_s = rows_a * LANES
    quota = spec_re.shape[2]
    sub = length_s // seq_count // LANES
    steps_a = jnp.arange(rows_a, dtype=jnp.int32)
    steps_b = jnp.arange(LANES, dtype=jnp.int32)
    last_re, last_im = unit_table(steps_b[:, None] * steps_b[None, :], LANES)
    u_re = rmul(spec_re, last_re) + rmul(spec_im, last_im)
    u_im = rmul(spec_im, last_re) - rmul(spec_re, last_im)
    tw_re, tw_im = unit_table(steps_a[:, None] * steps_b[None, :], length_s)
    tw_re = tw_re[:, None, None, :]
    tw_im = tw_im[:, None, None, :]
    u_re, u_im = (u_re * tw_re + u_im * tw_im, u_im * tw_re - u_re * tw_im)
    first_re, first_im = unit_table(steps_a[:, None] * steps_a[None, :], rows_a)
    out_re = lmul(first_re, u_re) + lmul(first_im, u_im)
    out_im = lmul(first_re, u_im) - lmul(first_im, u_re)
    both = jnp.stack([out_re, out_im], axis=0).reshape(2, seq_count, sub, 2, quota, LANES)
    recv = swap_leading(both.transpose(1, 3, 0, 2, 4, 5))
    recv = recv.reshape(2 * seq_count, 2, sub, quota, LANES)
    twist_re, twist_im = unit_table(slot_freq[:, None] * offsets[None, :], modulus)
    twist_re = twist_re.reshape(2 * seq_count, sub, 1, LANES)
    twist_im = twist_im.reshape(2 * seq_count, sub, 1, LANES)
    z_re = recv[:, 0]
    z_im = recv[:, 1]
    unt = jnp.stack(
        [z_re * twist_re + z_im * twist_im, z_im * twist_re - z_re * twist_im], axis=1
    )
    sources = jnp.arange(seq_count, dtype=jnp.int32)
    mix_re, mix_im = unit_table(sources[:, None] * slot_freq[None, :], 2 * seq_count)
    mix = jnp.stack([mix_re, mix_im], axis=-1).reshape(seq_count, 4 * seq_count)
    rows_out = lmul(mix, unt.reshape(4 * seq_count, sub, quota, LANES))
    back = swap_leading(rows_out)
    return back.transpose(2, 0, 1, 3).reshape(quota, length_s)


def local(out_grad, gate_act, conv_out, value_act, filter_taps, skip_gain):
    batch_rows = out_grad.shape[0]
    channels = out_grad.shape[1]
    length_s = out_grad.shape[2]
    seq_count = lax.axis_size("seq")
    row_total = batch_rows * channels
    stack_rows = 2 * row_total + 1
    blk = length_s // seq_count
    sub = blk // LANES
    rows_a = length_s // LANES
    modulus = 2 * seq_count * length_s
    slot_freq = row_order(seq_count)
    offsets = lax.axis_index("seq") * blk + jnp.arange(blk, dtype=jnp.int32)

    gated_rows = out_grad.astype(jnp.float32) * gate_act.astype(jnp.float32)
    gate_grad = (out_grad.astype(jnp.float32) * conv_out.astype(jnp.float32)).astype(jnp.bfloat16)
    stacked = jnp.concatenate(
        [
            gated_rows.reshape(row_total, length_s),
            value_act.astype(jnp.float32).reshape(row_total, length_s),
            filter_taps.reshape(1, length_s),
        ],
        axis=0,
    )
    recv1 = swap_leading(stacked.reshape(stack_rows, seq_count, blk).transpose(1, 0, 2))
    sources = jnp.arange(seq_count, dtype=jnp.int32)
    cross_re, cross_im = unit_table(slot_freq[:, None] * sources[None, :], 2 * seq_count)
    mixed = lmul(jnp.concatenate([cross_re, cross_im], axis=0), recv1)
    mixed = mixed.reshape(2, 2 * seq_count, stack_rows, blk)
    twist_re, twist_im = unit_table(slot_freq[:, None] * offsets[None, :], modulus)
    twist_re = twist_re[:, None, :]
    twist_im = twist_im[:, None, :]
    m_re = mixed[0]
    m_im = mixed[1]
    y = jnp.stack(
        [m_re * twist_re - m_im * twist_im, m_re * twist_im + m_im * twist_re], axis=0
    )
    y = y.reshape(2, seq_count, 2, stack_rows, sub, LANES).transpose(1, 4, 0, 2, 3, 5)
    recv2 = swap_leading(y)
    steps_a = jnp.arange(rows_a, dtype=jnp.int32)
    steps_b = jnp.arange(LANES, dtype=jnp.int32)
    first_re, first_im = unit_table(steps_a[:, None] * steps_a[None, :], rows_a)
    block = jnp.stack(
        [
            jnp.stack([first_re, -first_im], axis=-1),
            jnp.stack([first_im, first_re], axis=-1),
        ],
        axis=1,
    ).reshape(2 * rows_a, 2 * rows_a)
    y1 = lmul(block, recv2.reshape(2 * rows_a, 2 * stack_rows * LANES))
    y1 = y1.reshape(rows_a, 2, 2, stack_rows, LANES)
    tw_re, tw_im = unit_table(steps_a[:, None] * steps_b[None, :], length_s)
    tw_re = tw_re[:, None, None, :]
    tw_im = tw_im[:, None, None, :]
    y1_re = y1[:, 0]
    y1_im = y1[:, 1]
    y2_re = y1_re * tw_re - y1_im * tw_im
    y2_im = y1_re * tw_im + y1_im * tw_re
    last_re, last_im = unit_table(steps_b[:, None] * steps_b[None, :], LANES)
    spec_re = rmul(y2_re, last_re) - rmul(y2_im, last_im)
    spec_im = rmul(y2_re, last_im) + rmul(y2_im, last_re)
    grad_re = spec_re[:, :, :row_total]
    grad_im = spec_im[:, :, :row_total]
    value_re = spec_re[:, :, row_total : 2 * row_total]
    value_im = spec_im[:, :, row_total : 2 * row_total]
    filt_re = spec_re[:, :, 2 * row_total :]
    filt_im = spec_im[:, :, 2 * row_total :]
    carry_re = filt_re * grad_re + filt_im * grad_im
    carry_im = filt_re * grad_im - filt_im * grad_re
    lag_re = jnp.sum(grad_re * value_re + grad_im * value_im, axis=2, keepdims=True)
    lag_im = jnp.sum(grad_im * value_re - grad_re * value_im, axis=2, keepdims=True)
    lag_re, lag_im = lax.psum((lag_re, lag_im), "rep")
    rows_time = local_inverse(carry_re, carry_im, seq_count, slot_freq, offsets, modulus)
    lag_time = local_inverse(lag_re, lag_im, seq_count, slot_freq, offsets, modulus)
    inv_points = 1.0 / modulus
    carried = (rows_time * inv_points).reshape(batch_rows, channels, length_s)
    value_grad = (carried + skip_gain[None, :, None] * gated_rows).astype(jnp.bfloat16)
    norm_scale = 1.0 / math.sqrt(
        batch_rows * lax.axis_size("rep") * channels * length_s * seq_count
    )
    filter_grad = lag_time[0] * inv_points * norm_scale
    return (gate_grad, value_grad, filter_grad)


def solution(mesh):
    return jax.shard_map(
        local,
        mesh=mesh,
        in_specs=(
            P("rep", None, "seq"),
            P("rep", None, "seq"),
            P("rep", None, "seq"),
            P("rep", None, "seq"),
            P("seq"),
            P(),
        ),
        out_specs=(P("rep", None, "seq"), P("rep", None, "seq"), P("seq")),
        check_vma=False,
    )
```

time: 718 us -> 398 us (0.55)
  local copies, waits for them, and re-layouts: 296 us -> 44 us
  other arithmetic: 109 us -> 18.8 us
  waiting for transfers between devices: 162 us -> 218 us
  blocking collectives: 24.9 us -> 0 us
    unnamed x33 -> x18, local copies, waits for them, and re-layouts: 156 us -> 3.49 us
    unnamed x2 -> x0, other arithmetic: 74.5 us -> none
    all_to_all x5 -> x6, waiting for transfers between devices: 127 us -> 188 us  [swap_leading(): lax.all_to_all(values, 'seq', split_axis=0, concat_axis=0, tiled=True)]
    all_to_all x7 -> x2, local copies, waits for them, and re-layouts: 70.6 us -> 15.7 us  [swap_leading(): lax.all_to_all(values, 'seq', split_axis=0, concat_axis=0, tiled=True)]
    add x4 -> x0, local copies, waits for them, and re-layouts: 28.1 us -> none  [the longest x2 22.5 us: middle_complex(): out_im = middle_mix(table_im, left_re) + middle_mix(table_re, left_im)]
    sub x3 -> x0, local copies, waits for them, and re-layouts: 25 us -> none  [the longest x2 17.9 us: middle_complex(): out_re = middle_mix(table_re, left_re) - middle_mix(table_im, left_im)]
    all_to_all x1 -> x0, blocking collectives: 24.9 us -> none  [local(): lax.all_to_all(rows_out, 'seq', split_axis=1, concat_axis=2, tiled=True)]
    all_to_all x3 -> x0, other arithmetic: 23.9 us -> none  [the longest x1 8.94 us: local(): lax.all_to_all(back_re, 'seq', split_axis=2, concat_axis=1, tiled=True)]
  transfers between devices with their start and end apart: 6 -> 7, of which waited for: 4 -> 5; matrix products, arithmetic and copies ran while one was open for 19% -> 7% of each run, Pallas kernels for 0% -> 0%
where the time goes in v1:
time: 398 us; the launch traced here: 394 us
  waiting for transfers between devices  218 us (55%)
  matrix products  71.5 us (18%)
  local copies, waits for them, and re-layouts  44 us (11%)
  starting transfers between devices  26.3 us (7%)
  other arithmetic  18.8 us (5%)
  between operations  14.7 us (4%)
    all_to_all x6, waiting for transfers between devices, swap_leading(): lax.all_to_all(values, 'seq', split_axis=0, concat_axis=0, tiled=True)  188 us
    dot_general x12, matrix products, lmul(): return jnp.tensordot(table, values, axes=1, precision=HIGHEST)  39.5 us
    dot_general x12, matrix products, rmul(): return jnp.tensordot(values, table, axes=1, precision=HIGHEST)  32 us
    psum x1, waiting for transfers between devices, local(): lag_re, lag_im = lax.psum((lag_re, lag_im), 'rep')  29.9 us
    all_to_all x6, starting transfers between devices, swap_leading(): lax.all_to_all(values, 'seq', split_axis=0, concat_axis=0, tiled=True)  26.2 us
    all_to_all x2, local copies, waits for them, and re-layouts, swap_leading(): lax.all_to_all(values, 'seq', split_axis=0, concat_axis=0, tiled=True)  15.7 us
    dot_general x3, local copies, waits for them, and re-layouts, lmul(): return jnp.tensordot(table, values, axes=1, precision=HIGHEST)  11 us
    reshape x1, local copies, waits for them, and re-layouts, local(): y1 = lmul(block, recv2.reshape(2 * rows_a, 2 * stack_rows * LANES))  9.83 us
  transfers between devices with their start and end apart: 7, of which 5 were waited for; matrix products, arithmetic and copies ran while one was open for 7% of the time, Pallas kernels for 0%

profile of v1, /device:TPU:0, one launch (start us, length us, event | category | flops | bytes accessed | tf_op | source)
XLA Modules:
  0.0 393.7 jit_solution(10951180151788367974)
XLA Ops:
  12.5 5.4 %all-to-all-start = ((f32[8,33,2048]{2,1,0:T(8,128)}), f32[8,33,2048]{2,1,0:T(8,128)S(1)}, u32[]{:S(2)}, u32[]{:S(2)}) async-start(f32[8,33,2048]{2,1,0:T(8,128)} %copy.67), calls=%async_computation | async-start | bytes 5242880 | tf_op jit(solution)/shard_map/all_to_all | solution.py:33
  18.5 31.5 %all-to-all-done = f32[8,33,2048]{2,1,0:T(8,128)S(1)} async-done(((f32[8,33,2048]{2,1,0:T(8,128)}), f32[8,33,2048]{2,1,0:T(8,128)S(1)}, u32[]{:S(2)}, u32[]{:S(2)}) %all-to-all-start) | async-done | bytes 2162720 | tf_op jit(solution)/shard_map/all_to_all | solution.py:33
  50.1 7.7 %fusion.4 = f32[32,33,2048]{2,0,1:T(8,128)S(1)} fusion(f32[8,33,2048]{2,1,0:T(8,128)S(1)} %all-to-all-done, f32[16,8]{0,1:T(8,128)S(1)} %get-tuple-element.24, f32[16,8]{0,1:T(8,128)S(1)} %get-tuple-element.23), kind=kOutput, calls=%fused_computation.17 | convolution fusion | flops 207618304 | bytes 10814464 | tf_op jit(solution)/shard_map/dot_general | solution.py:25
  61.7 3.9 copy_bitcast_fusion
  65.6 5.2 %all-to-all-start.1 = ((f32[8,16,2,2,33,128]{5,1,4,3,2,0:T(8,128)}), f32[8,16,2,2,33,128]{5,1,4,3,2,0:T(8,128)}, u32[]{:S(2)}, u32[]{:S(2)}) async-start(f32[8,16,2,2,33,128]{5,1,4,3,2,0:T(8,128)} %copy_bitcast_fusion), calls=%async_computation.1 | async-start | bytes 17301504 | tf_op jit(solution)/shard_map/all_to_all | solution.py:33
  72.2 95.5 %all-to-all-done.1 = f32[8,16,2,2,33,128]{5,1,4,3,2,0:T(8,128)} async-done(((f32[8,16,2,2,33,128]{5,1,4,3,2,0:T(8,128)}), f32[8,16,2,2,33,128]{5,1,4,3,2,0:T(8,128)}, u32[]{:S(2)}, u32[]{:S(2)}) %all-to-all-start.1) | async-done | bytes 8650784 | tf_op jit(solution)/shard_map/all_to_all | solution.py:33
  167.7 10.3 %copy.71 = f32[8,16,2,2,33,128]{5,4,3,2,1,0:T(8,128)} copy(f32[8,16,2,2,33,128]{5,1,4,3,2,0:T(8,128)} %all-to-all-done.1) | data formatting | bytes 17301504 | tf_op jit(solution)/shard_map/all_to_all | solution.py:33
  178.0 9.8 %reshape.587 = f32[256,8448]{1,0:T(8,128)} reshape(f32[8,16,2,2,33,128]{5,4,3,2,1,0:T(8,128)} %copy.71) | data formatting | bytes 17301504 | tf_op jit(solution)/shard_map/reshape | solution.py:121
  187.8 9.2 %copy.72 = f32[8448,256]{1,0:T(8,128)} copy(f32[8448,256]{0,1:T(8,128)} %bitcast.148) | data formatting | bytes 17301504 | tf_op jit(solution)/shard_map/dot_general | solution.py:25
  196.9 11.4 %fusion.16 = f32[128,2,2,33,128]{4,0,3,2,1:T(8,128)S(1)} fusion(f32[2,33,128,256,1]{3,2,1,0,4:T(8,128)} %bitcast.147, f32[128,1,256]{2,0,1:T(8,128)S(1)} %copy.66, f32[128,1,256]{2,0,1:T(8,128)S(1)} %copy.65), kind=kOutput, calls=%fused_computation.49 | convolution fusion | flops 6643843072 | bytes 17563648 | tf_op jit(solution)/shard_map/dot_general | solution.py:25
  208.4 4.2 %fusion.11 = f32[128,2,33,128]{3,0,2,1:T(8,128)S(1)} fusion(f32[128,2,2,33,128]{4,0,3,2,1:T(8,128)S(1)} %fusion.16, f32[128,128]{1,0:T(8,128)S(1)} %get-tuple-element.27, f32[128,128]{1,0:T(8,128)S(1)} %get-tuple-element.28), kind=kOutput, calls=%fused_computation.43 | convolution fusion | flops 1664417792 | bytes 13107200 | tf_op jit(solution)/shard_map/dot_general | solution.py:29
  212.6 4.2 %fusion.10 = f32[128,2,33,128]{3,0,2,1:T(8,128)S(1)} fusion(f32[128,2,2,33,128]{4,0,3,2,1:T(8,128)S(1)} %fusion.16, f32[128,128]{1,0:T(8,128)S(1)} %get-tuple-element.27, f32[128,128]{1,0:T(8,128)S(1)} %get-tuple-element.28), kind=kOutput, calls=%fused_computation.42 | convolution fusion | flops 1664417792 | bytes 13107200 | tf_op jit(solution)/shard_map/dot_general | solution.py:29
  216.8 4.5 %convolution_subtract_fusion = f32[128,2,33,128]{3,0,2,1:T(8,128)S(1)} fusion(f32[128,2,33,128]{3,0,2,1:T(8,128)S(1)} %fusion.11, f32[128,2,2,33,128]{4,0,3,2,1:T(8,128)S(1)} %fusion.16, f32[128,128]{1,0:T(8,128)S(1)} %get-tuple-element.27, f32[128,128]{1,0:T(8,128)S(1)} %get-tuple-element.28), kind=kOutput, calls=%fused_computation.15 | convolution fusion | flops 1665499136 | bytes 17432576 | tf_op jit(solution)/shard_map/dot_general | solution.py:29
  221.3 4.3 %convolution_add_fusion = f32[128,2,33,128]{3,0,2,1:T(8,128)S(1)} fusion(f32[128,2,33,128]{3,0,2,1:T(8,128)S(1)} %fusion.10, f32[128,2,2,33,128]{4,0,3,2,1:T(8,128)S(1)} %fusion.16, f32[128,128]{1,0:T(8,128)S(1)} %get-tuple-element.27, f32[128,128]{1,0:T(8,128)S(1)} %get-tuple-element.28), kind=kOutput, calls=%fused_computation.14 | convolution fusion | flops 1665499136 | bytes 17432576 | tf_op jit(solution)/shard_map/dot_general | solution.py:29
  238.8 3.7 convolution_add_fusion.1
  242.5 5.2 %fusion.13 = f32[128,2,16,128]{3,0,2,1:T(8,128)} fusion(f32[128,2,16,128]{3,0,2,1:T(8,128)} %copy-done, f32[128,2,16,128]{3,0,2,1:T(8,128)S(1)} %convolution_subtract_fusion.2, f32[128,128]{1,0:T(8,128)S(1)} %get-tuple-element.27, f32[128,128]{1,0:T(8,128)S(1)} %get-tuple-element.28), kind=kOutput, calls=%fused_computation.45 | convolution fusion | flops 807108608 | bytes 6422528 | tf_op jit(solution)/shard_map/dot_general | solution.py:25
  247.7 29.9 %all-reduce.3.cloned.1.call-done = (f32[128,2,128]{2,0,1:T(8,128)}, f32[128,2,128]{2,0,1:T(8,128)}) async-done(((f32[128,2,128]{2,0,1:T(8,128)}, f32[128,2,128]{2,0,1:T(8,128)}), (f32[128,2,128]{2,0,1:T(8,128)}, f32[128,2,128]{2,0,1:T(8,128)})) %all-reduce.3.cloned.1.call-update) | async-done | bytes 262160 | tf_op jit(solution)/shard_map/psum | solution.py:143
  286.3 3.7 all-to-all-start.4
  290.0 4.6 %convolution_subtract_fusion.1 = f32[128,2,16,128]{3,0,2,1:T(8,128)S(1)} fusion(f32[128,2,16,128]{3,0,2,1:T(8,128)} %fusion.13, f32[128,2,16,128]{3,0,2,1:T(8,128)S(1)} %convolution_subtract_fusion.2, f32[128,2,16,128]{3,0,2,1:T(8,128)} %copy-done, f32[128,128]{1,0:T(8,128)S(1)} %get-tuple-element.27, f32[128,128]{1,0:T(8,128)S(1)} %get-tuple-element.28), kind=kOutput, calls=%fused_computation.27 | convolution fusion | flops 807632896 | bytes 8519680 | tf_op jit(solution)/shard_map/dot_general | solution.py:25
  297.2 4.6 %all-to-all-start.2 = ((f32[8,2,2,16,16,128]{5,3,4,1,2,0:T(8,128)}), f32[8,2,2,16,16,128]{5,3,4,1,2,0:T(8,128)}, u32[]{:S(2)}, u32[]{:S(2)}) async-start(f32[8,2,2,16,16,128]{5,3,4,1,2,0:T(8,128)} %copy_bitcast_fusion.1), calls=%async_computation.2 | async-start | bytes 8388608 | tf_op jit(solution)/shard_map/all_to_all | solution.py:33
  304.2 46.6 %all-to-all-done.2 = f32[8,2,2,16,16,128]{5,3,4,1,2,0:T(8,128)} async-done(((f32[8,2,2,16,16,128]{5,3,4,1,2,0:T(8,128)}), f32[8,2,2,16,16,128]{5,3,4,1,2,0:T(8,128)}, u32[]{:S(2)}, u32[]{:S(2)}) %all-to-all-start.2) | async-done | bytes 4194336 | tf_op jit(solution)/shard_map/all_to_all | solution.py:33
  354.2 5.4 %copy.75 = f32[8,2,2,16,16,128]{5,1,0,2,4,3:T(2,128)S(1)} copy(f32[8,2,2,16,16,128]{5,3,4,1,2,0:T(8,128)} %all-to-all-done.2) | data formatting | bytes 8388608 | tf_op jit(solution)/shard_map/all_to_all | solution.py:33
  363.5 4.1 %all-to-all-start.3 = ((f32[8,16,16,128]{3,2,1,0:T(8,128)}), f32[8,16,16,128]{3,2,1,0:T(8,128)S(1)}, u32[]{:S(2)}, u32[]{:S(2)}) async-start(f32[8,16,16,128]{3,2,1,0:T(8,128)} %copy.76), calls=%async_computation.3 | async-start | bytes 2097152 | tf_op jit(solution)/shard_map/all_to_all | solution.py:33
  368.3 14.8 %all-to-all-done.3 = f32[8,16,16,128]{3,2,1,0:T(8,128)S(1)} async-done(((f32[8,16,16,128]{3,2,1,0:T(8,128)}), f32[8,16,16,128]{3,2,1,0:T(8,128)S(1)}, u32[]{:S(2)}, u32[]{:S(2)}) %all-to-all-start.3) | async-done | bytes 1048608 | tf_op jit(solution)/shard_map/all_to_all | solution.py:33
  (76 shorter events, 49.4 us)
Async XLA Ops:
  7.2 2.0 copy-start.4
  8.5 1.0 copy-start.5
  12.5 37.6 %all-to-all-start = ((f32[8,33,2048]{2,1,0:T(8,128)}), f32[8,33,2048]{2,1,0:T(8,128)S(1)}, u32[]{:S(2)}, u32[]{:S(2)}) async-start(f32[8,33,2048]{2,1,0:T(8,128)} %copy.67), calls=%async_computation | async-start | bytes 5242880 | tf_op jit(solution)/shard_map/all_to_all | solution.py:33
  65.6 102.1 %all-to-all-start.1 = ((f32[8,16,2,2,33,128]{5,1,4,3,2,0:T(8,128)}), f32[8,16,2,2,33,128]{5,1,4,3,2,0:T(8,128)}, u32[]{:S(2)}, u32[]{:S(2)}) async-start(f32[8,16,2,2,33,128]{5,1,4,3,2,0:T(8,128)} %copy_bitcast_fusion), calls=%async_computation.1 | async-start | bytes 17301504 | tf_op jit(solution)/shard_map/all_to_all | solution.py:33
  70.8 206.7 %all-reduce.3.cloned.1.call-start = ((), (), s32[]{:S(2)}) async-start(), calls=%async_computation.6 | async-start | bytes 524288 | tf_op jit(solution)/shard_map/psum | solution.py:143
  236.5 2.3 copy-start
  286.3 10.8 %all-to-all-start.4 = ((f32[8,2,2,16,1,128]{5,3,2,1,4,0:T(8,128)}), f32[8,2,2,16,1,128]{5,3,2,1,4,0:T(8,128)S(1)}, u32[]{:S(2)}, u32[]{:S(2)}) async-start(f32[8,2,2,16,1,128]{5,3,2,1,4,0:T(8,128)} %copy_bitcast_fusion.2), calls=%async_computation.4 | async-start | bytes 524288 | tf_op jit(solution)/shard_map/all_to_all | solution.py:33
  290.0 4.6 %copy-start.1 = (f32[128,2,16,128]{3,0,2,1:T(8,128)S(1)}, f32[128,2,16,128]{3,0,2,1:T(8,128)}, u32[]{:S(2)}) copy-start(f32[128,2,16,128]{3,0,2,1:T(8,128)} %convolution_add_fusion.1) | copy-start | bytes 6291460
  297.2 53.7 %all-to-all-start.2 = ((f32[8,2,2,16,16,128]{5,3,4,1,2,0:T(8,128)}), f32[8,2,2,16,16,128]{5,3,4,1,2,0:T(8,128)}, u32[]{:S(2)}, u32[]{:S(2)}) async-start(f32[8,2,2,16,16,128]{5,3,4,1,2,0:T(8,128)} %copy_bitcast_fusion.1), calls=%async_computation.2 | async-start | bytes 8388608 | tf_op jit(solution)/shard_map/all_to_all | solution.py:33
  350.9 12.7 %all-to-all-start.5 = ((f32[8,16,1,128]{3,1,2,0:T(8,128)}), f32[8,16,1,128]{3,1,2,0:T(8,128)S(1)}, u32[]{:S(2)}, u32[]{:S(2)}) async-start(f32[8,16,1,128]{3,1,2,0:T(8,128)} %copy.83), calls=%async_computation.5 | async-start | bytes 131072 | tf_op jit(solution)/shard_map/all_to_all | solution.py:33
  363.5 19.5 %all-to-all-start.3 = ((f32[8,16,16,128]{3,2,1,0:T(8,128)}), f32[8,16,16,128]{3,2,1,0:T(8,128)S(1)}, u32[]{:S(2)}, u32[]{:S(2)}) async-start(f32[8,16,16,128]{3,2,1,0:T(8,128)} %copy.76), calls=%async_computation.3 | async-start | bytes 2097152 | tf_op jit(solution)/shard_map/all_to_all | solution.py:33
  383.2 1.0 copy-start.2
  383.2 1.2 copy-start.3
  383.2 1.2 copy-start.6
Sparse Core Ops, SparseCore 0:
  242.6 34.9 all-reduce.2
